TPU v7x, 512 devices: a whole 4x4x16 slice. The times are simulated.
512 devices in a mesh: ctx: 32 (over z, core), head: 16 (over x, y).
Axes of the slice: x: 4, y: 4, z: 16, core: 2. Of those that a mesh axis runs over, the one named last changes fastest.
Arguments:
- attn_q: bfloat16 [4096, 4096], P('ctx', 'head'), may hold values from -6 to 6
- attn_k: bfloat16 [4096, 512], P('ctx'), may hold values from -6 to 6
- attn_v: bfloat16 [4096, 512], P('ctx'), may hold values from -0.375 to 0.375
- attn_cot: bfloat16 [4096, 4096], P('ctx', 'head'), may hold values from -6 to 6
- attn_lse: float32 [16, 4096], P('head'), may hold values from 3 to 6
- attn_delta: float32 [16, 4096], P('head'), may hold values from -6 to 6
- block_lists: int32 [16, 64, 4], P('head'), may hold values from 0 to 63, as said below
- gdn_q: bfloat16 [4096, 2048], P('ctx', 'head'), may hold values from -6 to 6
- gdn_k: bfloat16 [4096, 2048], P('ctx', 'head'), may hold values from -6 to 6
- gdn_v: bfloat16 [4096, 4096], P('ctx', 'head'), may hold values from -6 to 6
- decay_logit: float32 [32, 4096], P('head', 'ctx'), may hold values from -8 to 8
- write_logit: float32 [32, 4096], P('head', 'ctx'), may hold values from -6 to 6
- decay_rate: float32 [32], P('head'), may hold values from 0.00024414062 to 0.1
- write_scale: float32 [32], P('head'), may hold values from 0.05 to 1
- gdn_cot: bfloat16 [4096, 4096], P('ctx', 'head'), may hold values from -6 to 6
Outputs:
- attn_dq: float32 [4096, 4096], P('ctx', 'head')
- attn_dk: float32 [4096, 512], P('ctx')
- attn_dv: float32 [4096, 512], P('ctx')
- gdn_dq: float32 [4096, 2048], P('ctx', 'head')
- gdn_dk: float32 [4096, 2048], P('ctx', 'head')
- gdn_dv: float32 [4096, 4096], P('ctx', 'head')
- gdn_ddecay: float32 [32, 4096], P('head', 'ctx')
- gdn_dwrite: float32 [32, 4096], P('head', 'ctx')
Inputs may be any that keep to these rules, and one draw needn't show every extreme that they name: `block_lists`: entries for query block b lie in 0 to b and may repeat.
All inputs are finite; a program needn't handle non-finite values.
Results may differ from a plain program's by a relative error of at most 0.00035.
Values may be sent and summed in bfloat16 or wider, within the bound.
No kernel may reach another device: no remote copies, remote signals or barrier semaphores. Data moves between devices by JAX's collectives and lax.ppermute only.
A program may use at most 128 MiB of HBM per device.

v0:
```python
import jax
import jax.numpy as jnp
from jax import lax
from jax.sharding import PartitionSpec as P

Q_HEADS = 16
KV_HEADS = 2
HD = 256
GDIM = 128
BLK = 64
TOPK = 4
SPAN = 64
HIGHEST = lax.Precision.HIGHEST


def prefix(value, axis, join, neutral, backward):
    count, mine = (lax.axis_size(axis), lax.axis_index(axis))
    pieces = jax.tree.map(lambda part: lax.all_gather(part, axis), value)
    if backward:
        pieces = jax.tree.map(lambda part: part[::-1], pieces)
        mine = count - 1 - mine
    so_far = jax.tree.map(
        lambda part, zero: jnp.full_like(part, 0) + jnp.asarray(zero, part.dtype), value, neutral
    )

    def turn(position, so_far):
        longer = join(so_far, jax.tree.map(lambda part: part[position], pieces))
        return jax.tree.map(lambda new, old: jnp.where(position < mine, new, old), longer, so_far)

    return lax.fori_loop(0, count - 1, turn, so_far)


def unit_rows(matrix):
    return matrix / jnp.sqrt(jnp.sum(matrix * matrix, axis=-1, keepdims=True) + 1e-06)


def span_update(memory, packed):
    queries, keys_in, values_in, log_decay, write_gain = packed
    length = log_decay.shape[-1]
    cum_log = jnp.cumsum(log_decay, axis=-1)
    log_gap = cum_log[:, :, None] - cum_log[:, None, :]
    order_ids = jnp.arange(length)
    strict_low = order_ids[:, None] > order_ids[None, :]
    with_diag = order_ids[:, None] >= order_ids[None, :]
    decay_strict = jnp.where(strict_low, jnp.exp(jnp.where(strict_low, log_gap, 0.0)), 0.0)
    decay_upto = jnp.where(with_diag, jnp.exp(jnp.where(with_diag, log_gap, 0.0)), 0.0)
    key_gram = jnp.einsum("htd,hsd->hts", keys_in, keys_in, precision=HIGHEST)
    system = write_gain[:, :, None] * decay_strict * key_gram + jnp.eye(length, dtype=jnp.float32)
    decay_now = jnp.exp(cum_log)
    recalled = jnp.einsum("hvd,htd->htv", memory, keys_in, precision=HIGHEST)
    target = write_gain[:, :, None] * (values_in - decay_now[:, :, None] * recalled)
    written = lax.linalg.triangular_solve(
        system, target, left_side=True, lower=True, unit_diagonal=True
    )
    read_old = jnp.einsum("hvd,htd->htv", memory, queries, precision=HIGHEST)
    query_key = jnp.einsum("htd,hsd->hts", queries, keys_in, precision=HIGHEST)
    outputs = decay_now[:, :, None] * read_old + jnp.einsum(
        "hts,hsv->htv", decay_upto * query_key, written, precision=HIGHEST
    )
    tail_decay = jnp.exp(cum_log[:, -1:] - cum_log)
    memory_next = jnp.exp(cum_log[:, -1])[:, None, None] * memory + jnp.einsum(
        "hsv,hsd->hvd", written * tail_decay[:, :, None], keys_in, precision=HIGHEST
    )
    return (memory_next, outputs)


def delta_forward(raw_inputs, memory, rate_heads, scale_heads):
    query_raw, key_raw, value_raw, decay_in, write_in = raw_inputs
    n_tokens = query_raw.shape[0]
    key_heads = query_raw.shape[1] // GDIM
    value_heads = value_raw.shape[1] // GDIM
    ratio_heads = value_heads // key_heads
    n_spans = n_tokens // SPAN
    queries = jnp.repeat(
        unit_rows(query_raw.reshape(n_tokens, key_heads, GDIM)), ratio_heads, axis=1
    )
    keys_norm = jnp.repeat(
        unit_rows(key_raw.reshape(n_tokens, key_heads, GDIM)), ratio_heads, axis=1
    )
    values_in = value_raw.reshape(n_tokens, value_heads, GDIM)
    log_decay = -rate_heads[:, None] * jax.nn.softplus(decay_in)
    write_gain = scale_heads[:, None] * jax.nn.sigmoid(write_in)

    def blocks_of(tensor):
        return tensor.reshape(n_spans, SPAN, value_heads, GDIM).transpose(0, 2, 1, 3)

    def gates_of(tensor):
        return tensor.reshape(value_heads, n_spans, SPAN).transpose(1, 0, 2)

    memory_end, outputs = lax.scan(
        span_update,
        memory,
        (
            blocks_of(queries),
            blocks_of(keys_norm),
            blocks_of(values_in),
            gates_of(log_decay),
            gates_of(write_gain),
        ),
    )
    return (outputs.transpose(0, 2, 1, 3).reshape(n_tokens, value_heads * GDIM), memory_end)


def sparse_query_grad(
    q_blocks,
    cot_blocks,
    own_keys,
    own_values,
    listed_keys,
    listed_values,
    lse_rows,
    delta_rows,
    head_lists,
    block_ids,
):
    score_scale = HD ** (-0.5)
    position = jnp.arange(BLK)
    causal = position[:, None] >= position[None, :]
    slot_ids = jnp.arange(TOPK)
    repeated = jnp.any(
        (head_lists[:, :, None] == head_lists[:, None, :])
        & (slot_ids[:, None] > slot_ids[None, :]),
        axis=2,
    )
    usable = (head_lists < block_ids[:, None]) & jnp.logical_not(repeated)
    own_score = (
        jnp.einsum("bid,bjd->bij", q_blocks, own_keys, preferred_element_type=jnp.float32)
        * score_scale
    )
    list_score = (
        jnp.einsum("bid,btjd->bitj", q_blocks, listed_keys, preferred_element_type=jnp.float32)
        * score_scale
    )
    own_prob = jnp.where(causal[None], jnp.exp(own_score - lse_rows[:, :, None]), 0.0)
    list_prob = jnp.where(
        usable[:, None, :, None], jnp.exp(list_score - lse_rows[:, :, None, None]), 0.0
    )
    own_dprob = jnp.einsum(
        "bid,bjd->bij", cot_blocks, own_values, preferred_element_type=jnp.float32
    )
    list_dprob = jnp.einsum(
        "bid,btjd->bitj", cot_blocks, listed_values, preferred_element_type=jnp.float32
    )
    own_dscore = own_prob * (own_dprob - delta_rows[:, :, None])
    list_dscore = list_prob * (list_dprob - delta_rows[:, :, None, None])
    own_part = jnp.einsum(
        "bij,bjd->bid", own_dscore, own_keys.astype(jnp.float32), precision=HIGHEST
    )
    list_part = jnp.einsum(
        "bitj,btjd->bid", list_dscore, listed_keys.astype(jnp.float32), precision=HIGHEST
    )
    return (own_part + list_part) * score_scale


def compose_maps(earlier, later):
    product = jnp.einsum("hij,hjk->hik", earlier[0], later[0], precision=HIGHEST)
    shifted = jnp.einsum("hij,hjk->hik", earlier[1], later[0], precision=HIGHEST) + later[1]
    return (product, shifted)


def on_device(
    attn_q,
    attn_k,
    attn_v,
    attn_cot,
    attn_lse,
    attn_delta,
    block_lists,
    gdn_q,
    gdn_k,
    gdn_v,
    decay_logit,
    write_logit,
    decay_rate,
    write_scale,
    gdn_cot,
):
    score_scale = HD ** (-0.5)
    head_index = lax.axis_index("head")
    ctx_index = lax.axis_index("ctx")
    tok_rows = attn_q.shape[0]
    local_heads = attn_q.shape[1] // HD
    blocks_here = tok_rows // BLK
    kv_group = head_index * local_heads // (Q_HEADS // KV_HEADS)
    own_keys = lax.dynamic_index_in_dim(
        attn_k.reshape(tok_rows, KV_HEADS, HD), kv_group, 1, keepdims=False
    )
    own_values = lax.dynamic_index_in_dim(
        attn_v.reshape(tok_rows, KV_HEADS, HD), kv_group, 1, keepdims=False
    )
    row_base = ctx_index * tok_rows
    first_block = ctx_index * blocks_here
    key_block_ids = first_block + jnp.arange(blocks_here, dtype=jnp.int32)
    member = jnp.any(block_lists[:, :, :, None] == key_block_ids[None, None, None, :], axis=2)
    member_rows = jnp.repeat(jnp.repeat(member, BLK, axis=1), BLK, axis=2)
    key_pos = row_base + jnp.arange(tok_rows, dtype=jnp.int32)
    key_block = key_pos // BLK
    keys_whole, values_whole = (
        lax.all_gather(own_keys, "ctx", axis=0, tiled=True),
        lax.all_gather(own_values, "ctx", axis=0, tiled=True),
    )
    lists_own = lax.dynamic_slice_in_dim(block_lists, first_block, blocks_here, 1)
    lse_own = lax.dynamic_slice_in_dim(attn_lse, row_base, tok_rows, 1).reshape(
        local_heads, blocks_here, BLK
    )
    delta_own = lax.dynamic_slice_in_dim(attn_delta, row_base, tok_rows, 1).reshape(
        local_heads, blocks_here, BLK
    )
    q_blocks = attn_q.reshape(blocks_here, BLK, local_heads, HD).transpose(2, 0, 1, 3)
    cot_blocks = attn_cot.reshape(blocks_here, BLK, local_heads, HD).transpose(2, 0, 1, 3)
    listed_keys = keys_whole.reshape(-1, BLK, HD)[lists_own]
    listed_values = values_whole.reshape(-1, BLK, HD)[lists_own]
    grad_blocks = jax.vmap(sparse_query_grad, in_axes=(0, 0, None, None, 0, 0, 0, 0, 0, None))(
        q_blocks,
        cot_blocks,
        own_keys.reshape(blocks_here, BLK, HD),
        own_values.reshape(blocks_here, BLK, HD),
        listed_keys,
        listed_values,
        lse_own,
        delta_own,
        lists_own,
        key_block_ids,
    )
    grad_q = grad_blocks.transpose(1, 2, 0, 3).reshape(tok_rows, local_heads * HD)
    query_rows = lax.all_gather(attn_q, "ctx", axis=0, tiled=True)
    n_rows = query_rows.shape[0]
    queries = query_rows.reshape(n_rows, local_heads, HD)
    cotangent = lax.all_gather(attn_cot, "ctx", axis=0, tiled=True).reshape(n_rows, local_heads, HD)
    row_pos = jnp.arange(n_rows, dtype=jnp.int32)
    row_block = row_pos // BLK
    own_pair = (row_block[:, None] == key_block[None, :]) & (row_pos[:, None] >= key_pos[None, :])
    listed_pair = member_rows & (key_block[None, :] < row_block[:, None])[None]
    allowed = own_pair[None] | listed_pair
    scores = (
        jnp.einsum("nhd,kd->hnk", queries, own_keys, preferred_element_type=jnp.float32)
        * score_scale
    )
    prob_full = jnp.where(allowed, jnp.exp(scores - attn_lse[:, :, None]), 0.0)
    dprobs = jnp.einsum("nhd,kd->hnk", cotangent, own_values, preferred_element_type=jnp.float32)
    dscores = prob_full * (dprobs - attn_delta[:, :, None])
    grad_value = jnp.einsum(
        "hnk,nhd->kd", prob_full, cotangent.astype(jnp.float32), precision=HIGHEST
    )
    grad_key = (
        jnp.einsum("hnk,nhd->kd", dscores, queries.astype(jnp.float32), precision=HIGHEST)
        * score_scale
    )
    slot_mask = (jnp.arange(KV_HEADS) == kv_group)[None, :, None]
    key_slots = jnp.where(slot_mask, grad_key[:, None, :], 0.0).reshape(tok_rows, KV_HEADS * HD)
    value_slots = jnp.where(slot_mask, grad_value[:, None, :], 0.0).reshape(tok_rows, KV_HEADS * HD)
    attn_dk, attn_dv = lax.psum((key_slots, value_slots), "head")
    raw_inputs = (
        gdn_q.astype(jnp.float32),
        gdn_k.astype(jnp.float32),
        gdn_v.astype(jnp.float32),
        decay_logit,
        write_logit,
    )
    value_heads = gdn_v.shape[1] // GDIM
    zero_memory = jnp.zeros((value_heads, GDIM, GDIM), jnp.float32)
    unit_memory = jnp.broadcast_to(jnp.eye(GDIM, dtype=jnp.float32), zero_memory.shape)

    def local_run(raw_values, memory):
        return delta_forward(raw_values, memory, decay_rate, write_scale)

    silent_inputs = (
        raw_inputs[0],
        raw_inputs[1],
        jnp.zeros_like(raw_inputs[2]),
        raw_inputs[3],
        raw_inputs[4],
    )
    transition = local_run(silent_inputs, unit_memory)[1]
    outputs_zero, pull_zero = jax.vjp(local_run, raw_inputs, zero_memory)
    written_end = outputs_zero[1]
    cot_full = gdn_cot.astype(jnp.float32)
    local_grad = pull_zero((cot_full, zero_memory))[1]
    memory_in = prefix(
        (transition, written_end), "ctx", compose_maps, (unit_memory, zero_memory), False
    )[1]
    flipped = jnp.swapaxes(transition, 1, 2)
    memory_grad = prefix(
        (flipped, local_grad), "ctx", compose_maps, (unit_memory, zero_memory), True
    )[1]
    unused_out, pull_final = jax.vjp(local_run, raw_inputs, memory_in)
    grads = pull_final((cot_full, memory_grad))[0]
    return (grad_q, attn_dk, attn_dv, grads[0], grads[1], grads[2], grads[3], grads[4])


def solution(mesh):
    return jax.shard_map(
        on_device,
        mesh=mesh,
        in_specs=(
            P("ctx", "head"),
            P("ctx", None),
            P("ctx", None),
            P("ctx", "head"),
            P("head", None),
            P("head", None),
            P("head", None, None),
            P("ctx", "head"),
            P("ctx", "head"),
            P("ctx", "head"),
            P("head", "ctx"),
            P("head", "ctx"),
            P("head"),
            P("head"),
            P("ctx", "head"),
        ),
        out_specs=(
            P("ctx", "head"),
            P("ctx", None),
            P("ctx", None),
            P("ctx", "head"),
            P("ctx", "head"),
            P("ctx", "head"),
            P("head", "ctx"),
            P("head", "ctx"),
        ),
        check_vma=False,
    )
```

profile of v0, /device:TPU:1, one launch (start us, length us, event | category | flops | bytes accessed | tf_op | source)
XLA Modules:
  0.0 767.3 jit_solution(10239268752019939677)
XLA Ops:
  20.4 24.4 %while.177 = (s32[]{:T(128)}, f32[2,128,128]{2,1,0:T(8,128)S(1)}, f32[2,2,64,1]{2,1,3,0:T(2,128)S(1)}, f32[2,2,64,1]{2,1,3,0:T(2,128)S(1)}, f32[2,2,64,64]{3,2,1...) while((s32[]{:T(128)}, f32[2,128,128]{2,1,0:T(8,128)S(1)}, ...), condition=%wide.region_11.13_spmd.clone.clone, body=%wide.region_9.12_spmd.clone.clone.sunk | while | flops 88404160 | bytes 1473784 | solution.py:90
  21.7 9.9 %custom-call.48 = f32[2,1,64,64]{2,3,1,0:T(8,128)S(1)} custom-call(f32[2,1,64,64]{3,2,1,0:T(8,128)S(1)} %add_bitcast_fusion.8), custom_call_target="InvertDiagBlocksLowerTriangular" | custom-call | tf_op jit(solution)/shard_map/jvp()/while/body/eval_jaxpr/triangular_solve/custom-call.1 | solution.py:52
  33.9 9.9 %custom-call.48 = f32[2,1,64,64]{2,3,1,0:T(8,128)S(1)} custom-call(f32[2,1,64,64]{3,2,1,0:T(8,128)S(1)} %add_bitcast_fusion.8), custom_call_target="InvertDiagBlocksLowerTriangular" | custom-call | tf_op jit(solution)/shard_map/jvp()/while/body/eval_jaxpr/triangular_solve/custom-call.1 | solution.py:52
  45.5 23.5 %while.174 = (s32[]{:T(128)}, f32[2,128,128]{2,1,0:T(8,128)S(1)}, f32[2,2,1,1]{1,3,2,0:T(1,128)S(1)}, f32[2,2,64,1]{2,1,3,0:T(2,128)S(1)}, f32[2,2,64,128]{3,2,1...) while((s32[]{:T(128)}, f32[2,128,128]{2,1,0:T(8,128)S(1)}, ...), condition=%wide.region_13.16_spmd.clone, body=%wide.region_12.15_spmd.clone.sunk | while | flops 100954176 | bytes 1590971 | solution.py:90
  46.3 9.8 %custom-call.47 = f32[2,1,64,64]{2,3,1,0:T(8,128)S(1)} custom-call(f32[2,1,64,64]{3,2,1,0:T(8,128)S(1)} %fusion.505), custom_call_target="InvertDiagBlocksLowerTriangular" | custom-call | tf_op jit(solution)/shard_map/transpose(jvp())/while/body/eval_jaxpr/triangular_solve/custom-call.0 | solution.py:52
  58.1 9.8 %custom-call.47 = f32[2,1,64,64]{2,3,1,0:T(8,128)S(1)} custom-call(f32[2,1,64,64]{3,2,1,0:T(8,128)S(1)} %fusion.505), custom_call_target="InvertDiagBlocksLowerTriangular" | custom-call | tf_op jit(solution)/shard_map/transpose(jvp())/while/body/eval_jaxpr/triangular_solve/custom-call.0 | solution.py:52
  69.9 23.7 %while.171 = (s32[]{:T(128)}, f32[2,128,128]{2,1,0:T(8,128)S(1)}, f32[2,2,64]{2,1,0:T(2,128)S(1)}, f32[2,2,64]{2,1,0:T(2,128)S(1)}, f32[2,2,64,128]{3,2,1,0:T(8,128)S(1)}, /*index=5*/s32[]{:T(128)}, f32[]{:T(128)}) while((s32[]{:T(128)}, f32[2,128,128]{2,1,0:T(8,128)S(1)}, f32[2,2,64]{2,1,0:T(2,128)S(1)}, f32[2,2,64]{2,1,0:T(2,128)S(1)}, ...), condition=%wide.region_7.9_spmd, body=%wide.region_5.8_spmd.sunk | while | flops 75726912 | bytes 1051785 | solution.py:90
  71.1 9.8 %custom-call.43 = f32[2,1,64,64]{2,3,1,0:T(8,128)S(1)} custom-call(f32[2,1,64,64]{3,2,1,0:T(8,128)S(1)} %fusion.440), custom_call_target="InvertDiagBlocksLowerTriangular" | custom-call | tf_op jit(solution)/shard_map/while/body/eval_jaxpr/triangular_solve/custom-call.1 | solution.py:52
  83.0 9.8 %custom-call.43 = f32[2,1,64,64]{2,3,1,0:T(8,128)S(1)} custom-call(f32[2,1,64,64]{3,2,1,0:T(8,128)S(1)} %fusion.440), custom_call_target="InvertDiagBlocksLowerTriangular" | custom-call | tf_op jit(solution)/shard_map/while/body/eval_jaxpr/triangular_solve/custom-call.1 | solution.py:52
  105.0 53.9 %all-gather.17.cloned.1.call-done = bf16[4096,256]{1,0:T(8,128)(2,1)} async-done(((bf16[128,256]{1,0:T(8,128)(2,1)}), bf16[4096,256]{1,0:T(8,128)(2,1)}) %all-gather.17.cloned.1.call-update) | async-done | bytes 2097168 | tf_op jit(solution)/shard_map/all_gather | solution.py:229
  165.2 66.4 %all-gather.21.cloned.1.call-done = bf16[4096,1,256]{0,2,1:T(8,128)(2,1)} async-done(((bf16[128,1,256]{0,2,1:T(8,128)(2,1)}), bf16[4096,1,256]{0,2,1:T(8,128)(2,1)}) %all-gather.21.cloned.1.call-update) | async-done | bytes 2097168 | tf_op jit(solution)/shard_map/all_gather | solution.py:200
  236.3 65.2 %all-gather.19.cloned.1.call-done = bf16[4096,1,256]{2,0,1:T(8,128)(2,1)} async-done(((bf16[128,1,256]{2,0,1:T(8,128)(2,1)}), bf16[4096,1,256]{2,0,1:T(8,128)(2,1)}) %all-gather.19.cloned.1.call-update) | async-done | bytes 2097168 | tf_op jit(solution)/shard_map/all_gather | solution.py:199
  308.2 65.6 %all-gather.25.cloned.1.call-done = f32[64,128,128]{2,1,0:T(8,128)} async-done(((f32[2,128,128]{2,1,0:T(8,128)}), f32[64,128,128]{2,1,0:T(8,128)}) %all-gather.25.cloned.1.call-update) | async-done | bytes 4194320 | tf_op jit(solution)/shard_map/all_gather | solution.py:18
  384.1 62.6 %all-gather.23.cloned.1.call-done = f32[64,128,128]{2,1,0:T(8,128)} async-done(((f32[2,128,128]{2,1,0:T(8,128)}), f32[64,128,128]{2,1,0:T(8,128)}) %all-gather.23.cloned.1.call-update) | async-done | bytes 4194320 | tf_op jit(solution)/shard_map/all_gather | solution.py:18
  456.9 40.1 %while.175 = (s32[]{:T(128)}, f32[2,128,128]{1,2,0:T(8,128)S(1)}, s32[]{:T(128)}, f32[32,2,128,128]{2,3,1,0:T(8,128)}, f32[32,2,128,128]{2,3,1,0:T(8,128)}, /*index=5*/s32[]{:T(128)}, s32[]{:T(128)}) while((s32[]{:T(128)}, f32[2,128,128]{1,2,0:T(8,128)S(1)}, s32[]{:T(128)}, f32[32,2,128,128]{2,3,1,0:T(8,128)}, ...), condition=%wide.region_15.18_spmd.clone, body=%wide.region_14.17_spmd.clone.sunk | while | flops 50462724 | bytes 920159 | solution.py:30
  497.2 21.8 %all-gather.29.cloned.1.call-done = f32[64,128,128]{2,1,0:T(8,128)} async-done(((f32[2,128,128]{2,1,0:T(8,128)}), f32[64,128,128]{2,1,0:T(8,128)}) %all-gather.29.cloned.1.call-update) | async-done | bytes 4194320 | tf_op jit(solution)/shard_map/all_gather | solution.py:18
  519.0 72.6 %all-gather.27.cloned.1.call-done = f32[64,128,128]{2,1,0:T(8,128)} async-done(((f32[2,128,128]{2,1,0:T(8,128)}), f32[64,128,128]{2,1,0:T(8,128)}) %all-gather.27.cloned.1.call-update) | async-done | bytes 4194320 | tf_op jit(solution)/shard_map/all_gather | solution.py:18
  591.6 73.7 %while.176 = (s32[]{:T(128)}, f32[2,128,128]{1,2,0:T(8,128)S(1)}, s32[]{:T(128)}, f32[32,2,128,128]{3,2,1,0:T(8,128)}, f32[32,2,128,128]{3,2,1,0:T(8,128)}, /*index=5*/s32[]{:T(128)}, s32[]{:T(128)}) while((s32[]{:T(128)}, f32[2,128,128]{1,2,0:T(8,128)S(1)}, s32[]{:T(128)}, f32[32,2,128,128]{3,2,1,0:T(8,128)}, ...), condition=%wide.region_17.20_spmd.clone, body=%wide.region_16.19_spmd.clone.sunk | while | flops 50462724 | bytes 1443939 | solution.py:30
  666.0 28.2 %while.172 = (s32[]{:T(128)}, f32[2,128,128]{2,1,0:T(8,128)S(1)}, f32[2,2,64,64]{3,2,1,0:T(8,128)S(1)}, f32[2,2,64,64]{3,2,1,0:T(8,128)S(1)}, f32[2,2,64,64]{3,2...) while((s32[]{:T(128)}, f32[2,128,128]{2,1,0:T(8,128)S(1)}, ...), condition=%wide.region_20.23_spmd.clone.clone, body=%wide.region_18.22_spmd.clone.clone.sunk | while | flops 113643840 | bytes 2896269 | solution.py:90
  667.4 9.8 %custom-call.44 = f32[2,1,64,64]{2,3,1,0:T(8,128)S(1)} custom-call(f32[2,1,64,64]{3,2,1,0:T(8,128)S(1)} %add_bitcast_fusion.6), custom_call_target="InvertDiagBlocksLowerTriangular" | custom-call | tf_op jit(solution)/shard_map/jvp()/while/body/eval_jaxpr/triangular_solve/custom-call.1 | solution.py:52
  681.4 9.8 %custom-call.44 = f32[2,1,64,64]{2,3,1,0:T(8,128)S(1)} custom-call(f32[2,1,64,64]{3,2,1,0:T(8,128)S(1)} %add_bitcast_fusion.6), custom_call_target="InvertDiagBlocksLowerTriangular" | custom-call | tf_op jit(solution)/shard_map/jvp()/while/body/eval_jaxpr/triangular_solve/custom-call.1 | solution.py:52
  694.3 54.4 %while.173 = (s32[]{:T(128)}, f32[2,128,128]{2,1,0:T(8,128)S(1)}, f32[2,2,64,128]{3,2,1,0:T(8,128)S(1)}, f32[2,2,64,128]{3,2,1,0:T(8,128)S(1)}, f32[2,2,64,128]{...) while((s32[]{:T(128)}, f32[2,128,128]{2,1,0:T(8,128)S(1)}, ...), condition=%wide.region_32.35_spmd.clone.clone, body=%wide.region_21.34_spmd.clone.clone.sunk | while | flops 258757312 | bytes 5322969 | solution.py:90
  695.7 9.8 %custom-call.46 = f32[2,1,64,64]{2,3,1,0:T(8,128)S(1)} custom-call(f32[2,1,64,64]{3,2,1,0:T(8,128)S(1)} %add_bitcast_fusion.7), custom_call_target="InvertDiagBlocksLowerTriangular" | custom-call | tf_op jit(solution)/shard_map/transpose(jvp())/while/body/eval_jaxpr/triangular_solve | solution.py:52
  706.0 9.8 %custom-call.45 = f32[2,1,64,64]{2,3,1,0:T(8,128)S(1)} custom-call(f32[2,1,64,64]{3,2,1,0:T(8,128)S(1)} %fusion.479), custom_call_target="InvertDiagBlocksLowerTriangular" | custom-call | tf_op jit(solution)/shard_map/transpose(jvp())/while/body/eval_jaxpr/triangular_solve/custom-call.0 | solution.py:52
  (608 shorter events, 242.1 us)
Async XLA Ops:
  7.2 95.0 %all-gather.15.cloned.1.call-start = ((), (), s32[]{:S(2)}) async-start(), calls=%async_computation | async-start | bytes 2162688 | tf_op jit(solution)/shard_map/all_gather | solution.py:226
  7.9 151.0 %all-gather.17.cloned.1.call-start = ((), (), s32[]{:S(2)}) async-start(), calls=%async_computation.1 | async-start | bytes 2162688 | tf_op jit(solution)/shard_map/all_gather | solution.py:229
  8.7 223.0 %all-gather.21.cloned.1.call-start = ((), (), s32[]{:S(2)}) async-start(), calls=%async_computation.3 | async-start | bytes 2162688 | tf_op jit(solution)/shard_map/all_gather | solution.py:200
  10.4 291.1 %all-gather.19.cloned.1.call-start = ((), (), s32[]{:S(2)}) async-start(), calls=%async_computation.2 | async-start | bytes 2162688 | tf_op jit(solution)/shard_map/all_gather | solution.py:199
  12.2 361.7 %all-gather.25.cloned.1.call-start = ((), (), s32[]{:S(2)}) async-start(), calls=%async_computation.5 | async-start | bytes 4325376 | tf_op jit(solution)/shard_map/all_gather | solution.py:18
  69.7 377.0 %all-gather.23.cloned.1.call-start = ((), (), s32[]{:S(2)}) async-start(), calls=%async_computation.4 | async-start | bytes 4325376 | tf_op jit(solution)/shard_map/all_gather | solution.py:18
  69.8 26.5 %copy-start.5 = (bf16[128,1,256]{0,2,1:T(8,128)(2,1)S(1)}, bf16[128,1,256]{0,2,1:T(8,128)(2,1)}, u32[]{:S(2)}) copy-start(bf16[128,1,256]{0,2,1:T(8,128)(2,1)} %constant_dynamic-slice_fusion.18) | copy-start | bytes 196612
  69.8 26.6 %copy-start.21 = (s32[1,64,4]{1,2,0:T(4,128)S(1)}, s32[1,64,4]{1,2,0:T(4,128)}, u32[]{:S(2)}) copy-start(s32[1,64,4]{1,2,0:T(4,128)} %param.39) | copy-start | bytes 3076
  69.8 27.8 %copy-start.31 = (f32[1,4096]{1,0:T(1,128)S(1)}, f32[1,4096]{1,0:T(1,128)}, u32[]{:S(2)}) copy-start(f32[1,4096]{1,0:T(1,128)} %param.37) | copy-start | bytes 49156
  69.8 27.9 %copy-start.20 = (f32[1,4096]{1,0:T(1,128)S(1)}, f32[1,4096]{1,0:T(1,128)}, u32[]{:S(2)}) copy-start(f32[1,4096]{1,0:T(1,128)} %param.38) | copy-start | bytes 49156
  69.8 31.3 %copy-start.6 = (bf16[128,1,256]{2,0,1:T(8,128)(2,1)S(1)}, bf16[128,1,256]{2,0,1:T(8,128)(2,1)}, u32[]{:S(2)}) copy-start(bf16[128,1,256]{2,0,1:T(8,128)(2,1)} %copy.214) | copy-start | bytes 196612
  69.9 31.3 %copy-start.15 = (bf16[128,256]{1,0:T(8,128)(2,1)S(1)}, bf16[128,256]{1,0:T(8,128)(2,1)}, u32[]{:S(2)}) copy-start(bf16[128,256]{1,0:T(8,128)(2,1)} %param.33) | copy-start | bytes 196612
  69.9 31.5 %copy-start.8 = (bf16[128,256]{1,0:T(8,128)(2,1)S(1)}, bf16[128,256]{1,0:T(8,128)(2,1)}, u32[]{:S(2)}) copy-start(bf16[128,256]{1,0:T(8,128)(2,1)} %param.36) | copy-start | bytes 196612
  94.4 424.6 %all-gather.29.cloned.1.call-start = ((), (), s32[]{:S(2)}) async-start(), calls=%async_computation.7 | async-start | bytes 4325376 | tf_op jit(solution)/shard_map/all_gather | solution.py:18
  95.2 496.5 %all-gather.27.cloned.1.call-start = ((), (), s32[]{:S(2)}) async-start(), calls=%async_computation.6 | async-start | bytes 4325376 | tf_op jit(solution)/shard_map/all_gather | solution.py:18
  95.9 661.5 %all-reduce.5.cloned.1.call-start = ((), (), s32[]{:S(2)}) async-start(), calls=%async_computation.8 | async-start | bytes 1048576 | tf_op jit(solution)/shard_map/psum | solution.py:252
  165.2 139.7 %copy-start.9 = (bf16[128,256]{1,0:T(8,128)(2,1)S(1)}, bf16[128,256]{1,0:T(8,128)(2,1)}, u32[]{:S(2)}) copy-start(bf16[128,256]{1,0:T(8,128)(2,1)} %param.36) | copy-start | bytes 196612
  236.3 70.2 %copy-start.16 = (f32[2,64,64]{1,2,0:T(8,128)S(1)}, f32[2,64,64]{1,2,0:T(8,128)}, u32[]{:S(2)}) copy-start(f32[2,64,64]{1,2,0:T(8,128)} %fusion.283) | copy-start | bytes 98308
  236.3 71.1 %copy-start.7 = (f32[16,8,2,256]{3,1,2,0:T(8,128)S(1)}, f32[16,8,2,256]{3,1,2,0:T(8,128)}, u32[]{:S(2)}) copy-start(f32[16,8,2,256]{3,1,2,0:T(8,128)} %copy.217) | copy-start | bytes 786436
  236.3 71.1 %copy-start.30 = (pred[512]{0:T(512)(128)(4,1)S(1)}, pred[512]{0:T(512)(128)(4,1)}, u32[]{:S(2)}) copy-start(pred[512]{0:T(512)(128)(4,1)} %broadcast_in_dim.479) | copy-start | bytes 1540
  666.0 28.2 %copy-start.14 = (pred[64,64]{1,0:T(8,128)(4,1)S(1)}, pred[64,64]{1,0:T(8,128)(4,1)}, u32[]{:S(2)}) copy-start(pred[64,64]{1,0:T(8,128)(4,1)} %iota_compare_fusion.16) | copy-start | bytes 12292
  694.2 54.5 %copy-start.10 = (bf16[128,128]{1,0:T(8,128)(2,1)S(1)}, bf16[128,128]{1,0:T(8,128)(2,1)}, u32[]{:S(2)}) copy-start(bf16[128,128]{1,0:T(8,128)(2,1)} %param.41) | copy-start | bytes 98308
  694.3 55.3 %copy-start.29 = (f32[128]{0:T(128)S(1)}, f32[128]{0:T(128)}, u32[]{:S(2)}) copy-start(f32[128]{0:T(128)} %copy-done.28) | copy-start | bytes 1540
  694.3 58.2 %copy-start.11 = (bf16[128,128]{1,0:T(8,128)(2,1)S(1)}, bf16[128,128]{1,0:T(8,128)(2,1)}, u32[]{:S(2)}) copy-start(bf16[128,128]{1,0:T(8,128)(2,1)} %param.40) | copy-start | bytes 98308
  (21 other events, 106.0 us)
Sparse Core Ops, SparseCore 0:
  10.1 79.2 all-gather.14
  91.5 67.3 all-gather.16
  161.5 70.0 all-gather.20
  234.2 67.3 all-gather.18
  303.5 70.3 all-gather.24
  376.4 70.1 all-gather.22
  448.8 70.1 all-gather.28
  521.1 70.4 all-gather.26
  595.5 111.3 all-reduce.4
where the time goes:
time: 770 us; the launch traced here: 767 us
  waiting for transfers between devices  411 us (53%)
  other arithmetic  142 us (18%)
  matrix products  114 us (15%)
  local copies, waits for them, and re-layouts  80.6 us (10%)
  between operations  14.9 us (2%)
    all_gather x4, waiting for transfers between devices, prefix(): pieces = jax.tree.map(lambda part: lax.all_gather(part, axis), value)  223 us
    another operation x44, other arithmetic, span_update(): lax.linalg.triangular_solve(system, target, left_side=True, lower=True, u...  119 us
    dot_general x62, matrix products, compose_maps(): jnp.einsum('hij,hjk->hik', earlier[1], later[0], precision=HIGHEST)  79.1 us
    all_gather x1, waiting for transfers between devices, on_device(): lax.all_gather(own_values, 'ctx', axis=0, tiled=True)  66.4 us
    all_gather x1, waiting for transfers between devices, on_device(): lax.all_gather(own_keys, 'ctx', axis=0, tiled=True)  65.2 us
    all_gather x1, waiting for transfers between devices, on_device(): lax.all_gather(attn_cot, 'ctx', axis=0, tiled=True)  53.9 us
    dynamic_slice x62, local copies, waits for them, and re-layouts, turn(): longer = join(so_far, jax.tree.map(lambda part: part[position], pieces))  31.4 us
  transfers between devices with their start and end apart: 9, of which 7 were waited for; matrix products, arithmetic and copies ran while one was open for 43% of the time, Pallas kernels for 0%

commit v1 on v0

--- a/solution.py
+++ b/solution.py
@@ -196,7 +196,9 @@
     key_pos = row_base + jnp.arange(tok_rows, dtype=jnp.int32)
     key_block = key_pos // BLK
     keys_whole, values_whole = (
-        lax.all_gather(own_keys, "ctx", axis=0, tiled=True),
+        jnp.concatenate(
+            lax.all_to_all(jnp.stack([own_keys] * lax.axis_size("ctx")), "ctx", 0, 0), axis=0
+        ),
         lax.all_gather(own_values, "ctx", axis=0, tiled=True),
     )
     lists_own = lax.dynamic_slice_in_dim(block_lists, first_block, blocks_here, 1)

time: 770 us -> 738 us (0.958)
  waiting for transfers between devices: 411 us -> 360 us
  starting transfers between devices: 0.54 us -> 17.4 us
    all_gather x1 -> x0, waiting for transfers between devices: 65.2 us -> none  [on_device(): lax.all_gather(own_keys, 'ctx', axis=0, tiled=True)]
    all_to_all x0 -> x1, starting transfers between devices: none -> 16.9 us  [on_device(): lax.all_to_all(jnp.stack([own_keys] * lax.axis_size('ctx')), 'ctx', 0, 0)]
    all_gather x1, waiting for transfers between devices: 53.9 us -> 64.4 us  [on_device(): lax.all_gather(attn_cot, 'ctx', axis=0, tiled=True)]
  transfers between devices with their start and end apart: 9 -> 9, of which waited for: 7 -> 6; matrix products, arithmetic and copies ran while one was open for 43% -> 45% of each run, Pallas kernels for 0% -> 0%
where the time goes in v1:
time: 738 us; the launch traced here: 735 us
  waiting for transfers between devices  360 us (49%)
  other arithmetic  144 us (20%)
  matrix products  115 us (16%)
  local copies, waits for them, and re-layouts  79.6 us (11%)
  starting transfers between devices  17.4 us (2%)
  between operations  15.1 us (2%)
    all_gather x4, waiting for transfers between devices, prefix(): pieces = jax.tree.map(lambda part: lax.all_gather(part, axis), value)  224 us
    another operation x44, other arithmetic, span_update(): lax.linalg.triangular_solve(system, target, left_side=True, lower=True, u...  119 us
    dot_general x62, matrix products, compose_maps(): jnp.einsum('hij,hjk->hik', earlier[1], later[0], precision=HIGHEST)  79.2 us
    all_gather x1, waiting for transfers between devices, on_device(): lax.all_gather(own_values, 'ctx', axis=0, tiled=True)  69 us
    all_gather x1, waiting for transfers between devices, on_device(): lax.all_gather(attn_cot, 'ctx', axis=0, tiled=True)  64.4 us
    dynamic_slice x62, local copies, waits for them, and re-layouts, turn(): longer = join(so_far, jax.tree.map(lambda part: part[position], pieces))  31.4 us
    all_to_all x1, starting transfers between devices, on_device(): lax.all_to_all(jnp.stack([own_keys] * lax.axis_size('ctx')), 'ctx', 0, 0)  16.9 us
  transfers between devices with their start and end apart: 9, of which 6 were waited for; matrix products, arithmetic and copies ran while one was open for 45% of the time, Pallas kernels for 0%

profile of v1, /device:TPU:1, one launch (start us, length us, event | category | flops | bytes accessed | tf_op | source)
XLA Modules:
  0.0 735.0 jit_solution(5084858875441547665)
XLA Ops:
  19.2 24.4 %while.177 = (s32[]{:T(128)}, f32[2,128,128]{2,1,0:T(8,128)S(1)}, f32[2,2,64,1]{2,1,3,0:T(2,128)S(1)}, f32[2,2,64,1]{2,1,3,0:T(2,128)S(1)}, f32[2,2,64,64]{3,2,1...) while((s32[]{:T(128)}, f32[2,128,128]{2,1,0:T(8,128)S(1)}, ...), condition=%wide.region_11.13_spmd.clone.clone, body=%wide.region_9.12_spmd.clone.clone.sunk | while | flops 88404160 | bytes 1473784 | solution.py:90
  20.5 9.8 %custom-call.48 = f32[2,1,64,64]{2,3,1,0:T(8,128)S(1)} custom-call(f32[2,1,64,64]{3,2,1,0:T(8,128)S(1)} %add_bitcast_fusion.8), custom_call_target="InvertDiagBlocksLowerTriangular" | custom-call | tf_op jit(solution)/shard_map/jvp()/while/body/eval_jaxpr/triangular_solve/custom-call.1 | solution.py:52
  32.7 9.8 %custom-call.48 = f32[2,1,64,64]{2,3,1,0:T(8,128)S(1)} custom-call(f32[2,1,64,64]{3,2,1,0:T(8,128)S(1)} %add_bitcast_fusion.8), custom_call_target="InvertDiagBlocksLowerTriangular" | custom-call | tf_op jit(solution)/shard_map/jvp()/while/body/eval_jaxpr/triangular_solve/custom-call.1 | solution.py:52
  44.3 23.5 %while.174 = (s32[]{:T(128)}, f32[2,128,128]{2,1,0:T(8,128)S(1)}, f32[2,2,1,1]{1,3,2,0:T(1,128)S(1)}, f32[2,2,64,1]{2,1,3,0:T(2,128)S(1)}, f32[2,2,64,128]{3,2,1...) while((s32[]{:T(128)}, f32[2,128,128]{2,1,0:T(8,128)S(1)}, ...), condition=%wide.region_13.16_spmd.clone, body=%wide.region_12.15_spmd.clone.sunk | while | flops 100954176 | bytes 1590971 | solution.py:90
  45.1 9.8 %custom-call.47 = f32[2,1,64,64]{2,3,1,0:T(8,128)S(1)} custom-call(f32[2,1,64,64]{3,2,1,0:T(8,128)S(1)} %fusion.505), custom_call_target="InvertDiagBlocksLowerTriangular" | custom-call | tf_op jit(solution)/shard_map/transpose(jvp())/while/body/eval_jaxpr/triangular_solve/custom-call.0 | solution.py:52
  56.9 9.8 %custom-call.47 = f32[2,1,64,64]{2,3,1,0:T(8,128)S(1)} custom-call(f32[2,1,64,64]{3,2,1,0:T(8,128)S(1)} %fusion.505), custom_call_target="InvertDiagBlocksLowerTriangular" | custom-call | tf_op jit(solution)/shard_map/transpose(jvp())/while/body/eval_jaxpr/triangular_solve/custom-call.0 | solution.py:52
  68.6 23.7 %while.171 = (s32[]{:T(128)}, f32[2,128,128]{2,1,0:T(8,128)S(1)}, f32[2,2,64]{2,1,0:T(2,128)S(1)}, f32[2,2,64]{2,1,0:T(2,128)S(1)}, f32[2,2,64,128]{3,2,1,0:T(8,128)S(1)}, /*index=5*/s32[]{:T(128)}, f32[]{:T(128)}) while((s32[]{:T(128)}, f32[2,128,128]{2,1,0:T(8,128)S(1)}, f32[2,2,64]{2,1,0:T(2,128)S(1)}, f32[2,2,64]{2,1,0:T(2,128)S(1)}, ...), condition=%wide.region_7.9_spmd, body=%wide.region_5.8_spmd.sunk | while | flops 75726912 | bytes 1051785 | solution.py:90
  69.9 9.9 %custom-call.43 = f32[2,1,64,64]{2,3,1,0:T(8,128)S(1)} custom-call(f32[2,1,64,64]{3,2,1,0:T(8,128)S(1)} %fusion.440), custom_call_target="InvertDiagBlocksLowerTriangular" | custom-call | tf_op jit(solution)/shard_map/while/body/eval_jaxpr/triangular_solve/custom-call.1 | solution.py:52
  81.7 9.8 %custom-call.43 = f32[2,1,64,64]{2,3,1,0:T(8,128)S(1)} custom-call(f32[2,1,64,64]{3,2,1,0:T(8,128)S(1)} %fusion.440), custom_call_target="InvertDiagBlocksLowerTriangular" | custom-call | tf_op jit(solution)/shard_map/while/body/eval_jaxpr/triangular_solve/custom-call.1 | solution.py:52
  96.3 16.9 %all-to-all-start = ((bf16[32,128,256]{2,1,0:T(8,128)(2,1)}), bf16[32,128,256]{2,1,0:T(8,128)(2,1)}, u32[]{:S(2)}, u32[]{:S(2)}) async-start(bf16[32,128,256]{2,1,0:T(8,128)(2,1)} %stack.5), calls=%async_computation | async-start | bytes 4194304 | tf_op jit(solution)/shard_map/all_to_all | solution.py:200
  124.3 64.4 %all-gather.15.cloned.1.call-done = bf16[4096,256]{1,0:T(8,128)(2,1)} async-done(((bf16[128,256]{1,0:T(8,128)(2,1)}), bf16[4096,256]{1,0:T(8,128)(2,1)}) %all-gather.15.cloned.1.call-update) | async-done | bytes 2097168 | tf_op jit(solution)/shard_map/all_gather | solution.py:231
  194.9 69.0 %all-gather.17.cloned.1.call-done = bf16[4096,1,256]{0,2,1:T(8,128)(2,1)} async-done(((bf16[128,1,256]{0,2,1:T(8,128)(2,1)}), bf16[4096,1,256]{0,2,1:T(8,128)(2,1)}) %all-gather.17.cloned.1.call-update) | async-done | bytes 2097168 | tf_op jit(solution)/shard_map/all_gather | solution.py:202
  270.4 67.2 %all-gather.21.cloned.1.call-done = f32[64,128,128]{2,1,0:T(8,128)} async-done(((f32[2,128,128]{2,1,0:T(8,128)}), f32[64,128,128]{2,1,0:T(8,128)}) %all-gather.21.cloned.1.call-update) | async-done | bytes 4194320 | tf_op jit(solution)/shard_map/all_gather | solution.py:18
  347.9 62.5 %all-gather.19.cloned.1.call-done = f32[64,128,128]{2,1,0:T(8,128)} async-done(((f32[2,128,128]{2,1,0:T(8,128)}), f32[64,128,128]{2,1,0:T(8,128)}) %all-gather.19.cloned.1.call-update) | async-done | bytes 4194320 | tf_op jit(solution)/shard_map/all_gather | solution.py:18
  420.7 40.2 %while.175 = (s32[]{:T(128)}, f32[2,128,128]{1,2,0:T(8,128)S(1)}, s32[]{:T(128)}, f32[32,2,128,128]{2,3,1,0:T(8,128)}, f32[32,2,128,128]{2,3,1,0:T(8,128)}, /*index=5*/s32[]{:T(128)}, s32[]{:T(128)}) while((s32[]{:T(128)}, f32[2,128,128]{1,2,0:T(8,128)S(1)}, s32[]{:T(128)}, f32[32,2,128,128]{2,3,1,0:T(8,128)}, ...), condition=%wide.region_15.18_spmd.clone, body=%wide.region_14.17_spmd.clone.sunk | while | flops 50462724 | bytes 920159 | solution.py:30
  461.0 22.2 %all-gather.25.cloned.1.call-done = f32[64,128,128]{2,1,0:T(8,128)} async-done(((f32[2,128,128]{2,1,0:T(8,128)}), f32[64,128,128]{2,1,0:T(8,128)}) %all-gather.25.cloned.1.call-update) | async-done | bytes 4194320 | tf_op jit(solution)/shard_map/all_gather | solution.py:18
  483.2 71.9 %all-gather.23.cloned.1.call-done = f32[64,128,128]{2,1,0:T(8,128)} async-done(((f32[2,128,128]{2,1,0:T(8,128)}), f32[64,128,128]{2,1,0:T(8,128)}) %all-gather.23.cloned.1.call-update) | async-done | bytes 4194320 | tf_op jit(solution)/shard_map/all_gather | solution.py:18
  555.1 73.7 %while.176 = (s32[]{:T(128)}, f32[2,128,128]{1,2,0:T(8,128)S(1)}, s32[]{:T(128)}, f32[32,2,128,128]{3,2,1,0:T(8,128)}, f32[32,2,128,128]{3,2,1,0:T(8,128)}, /*index=5*/s32[]{:T(128)}, s32[]{:T(128)}) while((s32[]{:T(128)}, f32[2,128,128]{1,2,0:T(8,128)S(1)}, s32[]{:T(128)}, f32[32,2,128,128]{3,2,1,0:T(8,128)}, ...), condition=%wide.region_17.20_spmd.clone, body=%wide.region_16.19_spmd.clone.sunk | while | flops 50462724 | bytes 1443939 | solution.py:30
  629.5 25.9 %while.172 = (s32[]{:T(128)}, f32[2,128,128]{2,1,0:T(8,128)S(1)}, f32[2,2,64,64]{3,2,1,0:T(8,128)S(1)}, f32[2,2,64,64]{3,2,1,0:T(8,128)S(1)}, f32[2,2,64,64]{3,2...) while((s32[]{:T(128)}, f32[2,128,128]{2,1,0:T(8,128)S(1)}, ...), condition=%wide.region_20.23_spmd.clone.clone, body=%wide.region_18.22_spmd.clone.clone.sunk | while | flops 113643840 | bytes 2896269 | solution.py:90
  630.8 9.8 %custom-call.44 = f32[2,1,64,64]{2,3,1,0:T(8,128)S(1)} custom-call(f32[2,1,64,64]{3,2,1,0:T(8,128)S(1)} %add_bitcast_fusion.6), custom_call_target="InvertDiagBlocksLowerTriangular" | custom-call | tf_op jit(solution)/shard_map/jvp()/while/body/eval_jaxpr/triangular_solve/custom-call.1 | solution.py:52
  643.8 9.8 %custom-call.44 = f32[2,1,64,64]{2,3,1,0:T(8,128)S(1)} custom-call(f32[2,1,64,64]{3,2,1,0:T(8,128)S(1)} %add_bitcast_fusion.6), custom_call_target="InvertDiagBlocksLowerTriangular" | custom-call | tf_op jit(solution)/shard_map/jvp()/while/body/eval_jaxpr/triangular_solve/custom-call.1 | solution.py:52
  656.1 54.4 %while.173 = (s32[]{:T(128)}, f32[2,128,128]{2,1,0:T(8,128)S(1)}, f32[2,2,64,128]{3,2,1,0:T(8,128)S(1)}, f32[2,2,64,128]{3,2,1,0:T(8,128)S(1)}, f32[2,2,64,128]{...) while((s32[]{:T(128)}, f32[2,128,128]{2,1,0:T(8,128)S(1)}, ...), condition=%wide.region_32.35_spmd.clone.clone, body=%wide.region_21.34_spmd.clone.clone.sunk | while | flops 258757312 | bytes 5289689 | solution.py:90
  657.5 9.8 %custom-call.46 = f32[2,1,64,64]{2,3,1,0:T(8,128)S(1)} custom-call(f32[2,1,64,64]{3,2,1,0:T(8,128)S(1)} %add_bitcast_fusion.7), custom_call_target="InvertDiagBlocksLowerTriangular" | custom-call | tf_op jit(solution)/shard_map/transpose(jvp())/while/body/eval_jaxpr/triangular_solve | solution.py:52
  684.7 9.8 %custom-call.46 = f32[2,1,64,64]{2,3,1,0:T(8,128)S(1)} custom-call(f32[2,1,64,64]{3,2,1,0:T(8,128)S(1)} %add_bitcast_fusion.7), custom_call_target="InvertDiagBlocksLowerTriangular" | custom-call | tf_op jit(solution)/shard_map/transpose(jvp())/while/body/eval_jaxpr/triangular_solve | solution.py:52
  (611 shorter events, 243.6 us)
Async XLA Ops:
  7.2 114.2 %all-gather.13.cloned.1.call-start = ((), (), s32[]{:S(2)}) async-start(), calls=%async_computation.1 | async-start | bytes 2162688 | tf_op jit(solution)/shard_map/all_gather | solution.py:228
  7.9 180.8 %all-gather.15.cloned.1.call-start = ((), (), s32[]{:S(2)}) async-start(), calls=%async_computation.2 | async-start | bytes 2162688 | tf_op jit(solution)/shard_map/all_gather | solution.py:231
  8.7 255.3 %all-gather.17.cloned.1.call-start = ((), (), s32[]{:S(2)}) async-start(), calls=%async_computation.3 | async-start | bytes 2162688 | tf_op jit(solution)/shard_map/all_gather | solution.py:202
  10.4 327.2 %all-gather.21.cloned.1.call-start = ((), (), s32[]{:S(2)}) async-start(), calls=%async_computation.5 | async-start | bytes 4325376 | tf_op jit(solution)/shard_map/all_gather | solution.py:18
  19.2 24.4 %copy-start.19 = (bf16[128,256]{1,0:T(8,128)(2,1)S(1)}, bf16[128,256]{1,0:T(8,128)(2,1)}, u32[]{:S(2)}) copy-start(bf16[128,256]{1,0:T(8,128)(2,1)} %param.47) | copy-start | bytes 196612
  68.5 341.9 %all-gather.19.cloned.1.call-start = ((), (), s32[]{:S(2)}) async-start(), calls=%async_computation.4 | async-start | bytes 4325376 | tf_op jit(solution)/shard_map/all_gather | solution.py:18
  68.6 25.9 %copy-start.18 = (bf16[128,512]{1,0:T(8,128)(2,1)S(1)}, bf16[128,512]{1,0:T(8,128)(2,1)}, u32[]{:S(2)}) copy-start(bf16[128,512]{1,0:T(8,128)(2,1)} %param.34) | copy-start | bytes 393220
  93.1 390.1 %all-gather.25.cloned.1.call-start = ((), (), s32[]{:S(2)}) async-start(), calls=%async_computation.7 | async-start | bytes 4325376 | tf_op jit(solution)/shard_map/all_gather | solution.py:18
  93.7 461.4 %all-gather.23.cloned.1.call-start = ((), (), s32[]{:S(2)}) async-start(), calls=%async_computation.6 | async-start | bytes 4325376 | tf_op jit(solution)/shard_map/all_gather | solution.py:18
  96.2 17.4 %copy-start.5 = (bf16[128,1,256]{0,2,1:T(8,128)(2,1)S(1)}, bf16[128,1,256]{0,2,1:T(8,128)(2,1)}, u32[]{:S(2)}) copy-start(bf16[128,1,256]{0,2,1:T(8,128)(2,1)} %constant_dynamic-slice_fusion.18) | copy-start | bytes 196612
  96.2 17.5 %copy-start.22 = (s32[1,64,4]{1,2,0:T(4,128)S(1)}, s32[1,64,4]{1,2,0:T(4,128)}, u32[]{:S(2)}) copy-start(s32[1,64,4]{1,2,0:T(4,128)} %param.39) | copy-start | bytes 3076
  96.2 24.1 %copy-start.14 = (bf16[128,256]{1,0:T(8,128)(2,1)S(1)}, bf16[128,256]{1,0:T(8,128)(2,1)}, u32[]{:S(2)}) copy-start(bf16[128,256]{1,0:T(8,128)(2,1)} %param.33) | copy-start | bytes 196612
  96.3 24.3 %copy-start.7 = (bf16[128,256]{1,0:T(8,128)(2,1)S(1)}, bf16[128,256]{1,0:T(8,128)(2,1)}, u32[]{:S(2)}) copy-start(bf16[128,256]{1,0:T(8,128)(2,1)} %param.36) | copy-start | bytes 196612
  96.3 621.5 %all-to-all-start = ((bf16[32,128,256]{2,1,0:T(8,128)(2,1)}), bf16[32,128,256]{2,1,0:T(8,128)(2,1)}, u32[]{:S(2)}, u32[]{:S(2)}) async-start(bf16[32,128,256]{2,1,0:T(8,128)(2,1)} %stack.5), calls=%async_computation | async-start | bytes 4194304 | tf_op jit(solution)/shard_map/all_to_all | solution.py:200
  113.2 611.6 %all-reduce.5.cloned.1.call-start = ((), (), s32[]{:S(2)}) async-start(), calls=%async_computation.8 | async-start | bytes 1048576 | tf_op jit(solution)/shard_map/psum | solution.py:254
  121.3 67.3 %copy-start.21 = (f32[1,4096]{1,0:T(1,128)S(1)}, f32[1,4096]{1,0:T(1,128)}, u32[]{:S(2)}) copy-start(f32[1,4096]{1,0:T(1,128)} %param.38) | copy-start | bytes 49156
  629.5 26.6 %copy-start.13 = (pred[64,64]{1,0:T(8,128)(4,1)S(1)}, pred[64,64]{1,0:T(8,128)(4,1)}, u32[]{:S(2)}) copy-start(pred[64,64]{1,0:T(8,128)(4,1)} %iota_compare_fusion.16) | copy-start | bytes 12292
  656.1 54.7 %copy-start.8 = (bf16[128,128]{1,0:T(8,128)(2,1)S(1)}, bf16[128,128]{1,0:T(8,128)(2,1)}, u32[]{:S(2)}) copy-start(bf16[128,128]{1,0:T(8,128)(2,1)} %param.41) | copy-start | bytes 98308
  656.1 55.6 %copy-start.9 = (bf16[128,128]{1,0:T(8,128)(2,1)S(1)}, bf16[128,128]{1,0:T(8,128)(2,1)}, u32[]{:S(2)}) copy-start(bf16[128,128]{1,0:T(8,128)(2,1)} %param.40) | copy-start | bytes 98308
  656.1 22.7 %copy-start.33 = (f32[2,2,1,1]{1,3,2,0:T(1,128)}, f32[2,2,1,1]{1,3,2,0:T(1,128)S(1)}, u32[]{:S(2)}) copy-start(f32[2,2,1,1]{1,3,2,0:T(1,128)S(1)} %get-tuple-element.4409) | copy-start | bytes 52 | tf_op jit(solution)/shard_map/transpose(jvp())/while
  683.3 22.7 %copy-start.33 = (f32[2,2,1,1]{1,3,2,0:T(1,128)}, f32[2,2,1,1]{1,3,2,0:T(1,128)S(1)}, u32[]{:S(2)}) copy-start(f32[2,2,1,1]{1,3,2,0:T(1,128)S(1)} %get-tuple-element.4409) | copy-start | bytes 52 | tf_op jit(solution)/shard_map/transpose(jvp())/while
  710.5 11.9 %copy-start.10 = (f32[2,2,64,128]{3,2,1,0:T(8,128)S(1)}, f32[2,2,64,128]{3,2,1,0:T(8,128)}, u32[]{:S(2)}) copy-start(f32[2,2,64,128]{3,2,1,0:T(8,128)} %get-tuple-element.2079) | copy-start | bytes 393220
  710.5 12.6 %copy-start.25 = (f32[128]{0:T(128)S(1)}, f32[128]{0:T(128)}, u32[]{:S(2)}) copy-start(f32[128]{0:T(128)} %copy-done.24) | copy-start | bytes 1540
  710.5 13.4 %copy-start.15 = (f32[2,64,64]{1,2,0:T(8,128)S(1)}, f32[2,64,64]{1,2,0:T(8,128)}, u32[]{:S(2)}) copy-start(f32[2,64,64]{1,2,0:T(8,128)} %fusion.283) | copy-start | bytes 98308
  (22 other events, 61.5 us)
Sparse Core Ops, SparseCore 0:
  10.1 78.4 all-gather.12
  90.8 97.8 all-gather.14
  191.3 72.5 all-gather.16
  266.5 71.1 all-gather.20
  340.2 70.1 all-gather.18
  412.4 70.7 all-gather.24
  485.3 69.7 all-gather.22
  558.9 111.2 all-reduce.4
